TPU v7x, 256 devices: a whole 4x4x8 slice. The times are simulated.
256 devices in a mesh: expert: 16 (over y_hi, z), mp: 8 (over y_lo, x), batch: 2 (over core).
Axes of the slice: x: 4, y: 4 (y_hi: 2, y_lo: 2; y = y_hi * 2 + y_lo), z: 8, core: 2. Of those that a mesh axis runs over, the one named last changes fastest.
Arguments:
- tokens: bfloat16 [2, 2048, 2880], P('batch', 'expert', 'mp'), may hold values from -6 to 6
- segments: int32 [2, 2048], P('batch'), may hold values from 0 to 63, never falling along the last dimension, each value on 1 to 1024 neighbouring positions
- attn_gain: float32 [2880], replicated, may hold values from 0.6 to 9
- w_query: bfloat16 [2880, 4096], P('expert', 'mp'), may hold values from -0.109375 to 0.109375
- key_weight: bfloat16 [2880, 512], P('expert', 'mp'), may hold values from -0.109375 to 0.109375
- value_weight: bfloat16 [2880, 512], P('expert', 'mp'), may hold values from -0.109375 to 0.109375
- w_out: bfloat16 [4096, 2880], P('mp', 'expert'), may hold values from -0.09375 to 0.09375
- sink_head_logit: float32 [64], P('mp'), may hold values from -4 to 4
- moe_gain: float32 [2880], replicated, may hold values from 0.5 to 1.5
- expert_in: bfloat16 [16, 2, 2880, 2880], P('expert', None, None, 'mp'), may hold values from -0.3125 to 0.3125
- expert_down: bfloat16 [16, 2880, 2880], P('expert', 'mp'), may hold values from -0.01953125 to 0.01953125
- routes: int32 [2, 2048, 4], P('batch', 'expert'), may hold values from 0 to 15, all different within a row; in each aligned block of 128 rows (0 to 127, 128 to 255, ..., all dimensions but the last counted through in order) at most 48 rows name the same one
- route_weights: float32 [2, 2048, 4], P('batch', 'expert'), may hold values from 0.1 to 1
Outputs:
- hidden: bfloat16 [2, 2048, 2880], P('batch', 'expert', 'mp')
- key_cache: bfloat16 [2, 2048, 512], P('batch', 'expert', 'mp')
- value_cache: bfloat16 [2, 2048, 512], P('batch', 'expert', 'mp')
Inputs may be any that keep to these rules, and one draw needn't show every extreme that they name: Within each aligned block of 128 tokens of a micro-batch (the tokens of one index of expert), no expert is named by more than 48 routes; a token's routes name different experts. `segments`: segment numbers never fall along a micro-batch; one segment holds at most 1024 tokens.
All inputs are finite; a program needn't handle non-finite values.
Results may differ from a plain program's by a relative error of at most 0.024.
The roundings to bfloat16 on the way count: a program that leaves them out, or rounds other values in their place, can miss the bound.
Values may be sent and summed in bfloat16 or wider, within the bound.
No kernel may reach another device: no remote copies, remote signals or barrier semaphores. Data moves between devices by JAX's collectives and lax.ppermute only.
A program may use at most 64 MiB of HBM per device.

v0:
```python
import math
import jax
import jax.numpy as jnp
from jax import lax
from jax.sharding import PartitionSpec as P

HEAD_SIZE = 64
eps = 1e-05
rope_base = 150000.0
clamp_limit = 7.0
glu_alpha = 1.702


def rms_norm(row_block, gain):
    values = row_block.astype(jnp.float32)
    inv_scale = lax.rsqrt(jnp.mean(values * values, axis=-1, keepdims=True) + eps)
    return (values * inv_scale * gain).astype(jnp.bfloat16)


def apply_rotary(values, token_positions):
    half_dim = values.shape[-1] // 2
    inv_freq = jnp.power(
        rope_base, -2.0 * jnp.arange(half_dim, dtype=jnp.float32) / values.shape[-1]
    )
    rot_angle = token_positions.astype(jnp.float32)[:, None] * inv_freq[None, :]
    cosine = jnp.cos(rot_angle)[:, None, :]
    sine_val = jnp.sin(rot_angle)[:, None, :]
    first_half = values[..., :half_dim]
    second_half = values[..., half_dim:]
    return jnp.concatenate(
        [
            first_half * cosine - second_half * sine_val,
            second_half * cosine + first_half * sine_val,
        ],
        axis=-1,
    )


def gather_by_exchange(block, axis_name):
    count = lax.axis_size(axis_name)
    spread = jnp.broadcast_to(block[None], (count,) + block.shape)
    got = lax.all_to_all(spread, axis_name, split_axis=0, concat_axis=0, tiled=True)
    return got.reshape((count * block.shape[0],) + block.shape[1:])


def expert_rows(row_block, w_in, w_down):
    gate_val = jnp.dot(row_block, w_in[0], preferred_element_type=jnp.float32)
    up_val = jnp.dot(row_block, w_in[1], preferred_element_type=jnp.float32)
    gate_val = jnp.minimum(gate_val, clamp_limit)
    up_val = jnp.clip(up_val, -clamp_limit, clamp_limit)
    activated = ((up_val + 1.0) * gate_val * jax.nn.sigmoid(glu_alpha * gate_val)).astype(
        jnp.bfloat16
    )
    return jnp.dot(activated, w_down, preferred_element_type=jnp.float32)


def shards(
    tokens,
    segments,
    attn_gain,
    w_query,
    key_weight,
    value_weight,
    w_out,
    sink_head_logit,
    moe_gain,
    expert_in,
    expert_down,
    routes,
    route_weights,
):
    local_rows = tokens[0]
    tok_count = local_rows.shape[0]
    expert_devs = lax.axis_size("expert")
    row_start = lax.axis_index("expert") * tok_count
    mp_devs = lax.axis_size("mp")
    whole_rows = gather_by_exchange(local_rows.T, "mp").reshape(-1, tok_count).T
    input_normalised = rms_norm(whole_rows, attn_gain)
    query_cols = w_query.shape[1]
    kv_cols = key_weight.shape[1]
    shard_rows = w_query.shape[0]
    padded_rows = -(-shard_rows // 8) * 8
    big_weights = lax.all_gather(
        jnp.pad(
            jnp.concatenate([w_query, w_out.T], axis=1), ((0, padded_rows - shard_rows), (0, 0))
        ),
        "expert",
        axis=0,
    )
    query_weight = big_weights[:, :, :query_cols].reshape(expert_devs * padded_rows, query_cols)
    out_weight_t = big_weights[:, :, query_cols:]
    kv_weight = gather_by_exchange(jnp.concatenate([key_weight, value_weight], axis=1), "expert")
    normed_padded = jnp.pad(
        input_normalised.reshape(tok_count, expert_devs, shard_rows),
        ((0, 0), (0, 0), (0, padded_rows - shard_rows)),
    ).reshape(tok_count, expert_devs * padded_rows)
    query_raw = jnp.dot(normed_padded, query_weight, preferred_element_type=jnp.float32)
    kv_raw = jnp.dot(input_normalised, kv_weight, preferred_element_type=jnp.float32)
    key_raw = kv_raw[:, :kv_cols]
    value_raw = kv_raw[:, kv_cols:]
    token_positions = row_start + jnp.arange(tok_count, dtype=jnp.int32)
    query_by_head = query_cols // HEAD_SIZE
    kv_heads = kv_cols // HEAD_SIZE
    heads_per_group = query_by_head // kv_heads
    query_matrix = apply_rotary(
        query_raw.reshape(tok_count, query_by_head, HEAD_SIZE), token_positions
    ).astype(jnp.bfloat16)
    key_rotary = (
        apply_rotary(key_raw.reshape(tok_count, kv_heads, HEAD_SIZE), token_positions)
        .astype(jnp.bfloat16)
        .reshape(tok_count, kv_cols)
    )
    value_fresh = value_raw.astype(jnp.bfloat16)
    kv_all = gather_by_exchange(jnp.concatenate([key_rotary, value_fresh], axis=1), "expert")
    keys_all = kv_all[:, :kv_cols]
    values_all = kv_all[:, kv_cols:]
    seq_len = keys_all.shape[0]
    seg_all = segments[0]
    seg_local = lax.dynamic_slice_in_dim(seg_all, row_start, tok_count)
    row_total = heads_per_group * tok_count
    query_rows = (
        query_matrix.reshape(tok_count, kv_heads, heads_per_group, HEAD_SIZE)
        .transpose(1, 2, 0, 3)
        .reshape(kv_heads, row_total, HEAD_SIZE)
    )
    key_by_head = keys_all.reshape(seq_len, kv_heads, HEAD_SIZE).transpose(1, 0, 2)
    value_by_head = values_all.reshape(seq_len, kv_heads, HEAD_SIZE).transpose(1, 0, 2)
    row_pos = jnp.tile(token_positions, heads_per_group)
    row_seg = jnp.tile(seg_local, heads_per_group)
    sink_rows = jnp.repeat(sink_head_logit.reshape(kv_heads, heads_per_group), tok_count, axis=1)
    key_block = math.gcd(seq_len, 2048)
    block_count = seq_len // key_block
    score_scale = HEAD_SIZE ** (-0.5)

    def block_scores(index):
        key_first = index * key_block
        key_part = lax.dynamic_slice_in_dim(key_by_head, key_first, key_block, 1)
        scores = (
            jnp.einsum("hrd,hkd->hrk", query_rows, key_part, preferred_element_type=jnp.float32)
            * score_scale
        )
        key_pos = key_first + jnp.arange(key_block, dtype=jnp.int32)
        key_seg = lax.dynamic_slice_in_dim(seg_all, key_first, key_block, 0)
        allowed = (key_pos[None, :] <= row_pos[:, None]) & (key_seg[None, :] == row_seg[:, None])
        return jnp.where(allowed[None], scores, -jnp.inf)

    def max_step(index, running):
        return jnp.maximum(running, jnp.max(block_scores(index), axis=-1))

    row_max = lax.fori_loop(0, block_count, max_step, sink_rows)

    def sum_step(index, carried):
        weighted, denom = carried
        probs = jnp.exp(block_scores(index) - row_max[..., None]).astype(jnp.bfloat16)
        value_part = lax.dynamic_slice_in_dim(value_by_head, index * key_block, key_block, 1)
        weighted = weighted + jnp.einsum(
            "hrk,hkd->hrd", probs, value_part, preferred_element_type=jnp.float32
        )
        denom = denom + jnp.sum(probs, axis=-1, dtype=jnp.float32)
        return (weighted, denom)

    init_pair = (
        jnp.zeros((kv_heads, row_total, HEAD_SIZE), jnp.float32),
        jnp.zeros((kv_heads, row_total), jnp.float32),
    )
    weighted, denom = lax.fori_loop(0, block_count, sum_step, init_pair)
    denom = denom + jnp.exp(sink_rows - row_max)
    mixed = (weighted / denom[..., None]).astype(jnp.bfloat16)
    mixed = (
        mixed.reshape(kv_heads, heads_per_group, tok_count, HEAD_SIZE)
        .transpose(2, 0, 1, 3)
        .reshape(tok_count, query_cols)
    )
    out_terms_t = jnp.einsum(
        "efc,tc->eft", out_weight_t, mixed, preferred_element_type=jnp.float32
    )[:, :shard_rows]
    model_width = out_terms_t.shape[0] * out_terms_t.shape[1]
    out_pieces = out_terms_t.astype(jnp.bfloat16).reshape(
        mp_devs, model_width // mp_devs, tok_count
    )
    out_got = lax.all_to_all(out_pieces, "mp", split_axis=0, concat_axis=0, tiled=True)
    attn_part = jnp.sum(out_got.astype(jnp.float32), axis=0).T
    first_out = (local_rows.astype(jnp.float32) + attn_part).astype(jnp.bfloat16)
    top_count = routes.shape[2]
    local_experts = expert_in.shape[0]
    expert_count = local_experts * expert_devs
    capacity = 3 * tok_count * top_count // (2 * expert_count)
    chosen = routes[0].reshape(tok_count * top_count)
    onehot = (chosen[:, None] == jnp.arange(expert_count, dtype=jnp.int32)[None, :]).astype(
        jnp.int32
    )
    ranks = jnp.sum((jnp.cumsum(onehot, axis=0) - onehot) * onehot, axis=1)
    target = chosen * capacity + ranks
    source_row = (
        jnp.full((expert_count * capacity,), tok_count, jnp.int32)
        .at[target]
        .set(jnp.arange(tok_count * top_count, dtype=jnp.int32) // top_count)
    )
    padded = jnp.concatenate([first_out, jnp.zeros((1, first_out.shape[1]), jnp.bfloat16)], axis=0)
    pick = (source_row[:, None] == jnp.arange(tok_count + 1, dtype=jnp.int32)[None, :]).astype(
        jnp.bfloat16
    )
    outgoing = (
        jnp.dot(pick, padded, preferred_element_type=jnp.float32)
        .astype(jnp.bfloat16)
        .reshape(expert_count, capacity, padded.shape[1])
    )
    arrived = lax.all_to_all(outgoing, "expert", split_axis=0, concat_axis=0, tiled=True)
    arrived_rows = arrived.reshape(expert_count * capacity, arrived.shape[2])
    inputs = rms_norm(lax.all_gather(arrived_rows, "mp", axis=1, tiled=True), moe_gain)
    w_in = expert_in[0]
    hidden_cols = w_in.shape[2]
    inputs = lax.optimization_barrier(inputs)
    gate_up = jnp.dot(
        inputs, jnp.concatenate([w_in[0], w_in[1]], axis=1), preferred_element_type=jnp.float32
    )
    gate_val = gate_up[:, :hidden_cols]
    up_val = gate_up[:, hidden_cols:]
    gate_val = jnp.minimum(gate_val, clamp_limit)
    up_val = jnp.clip(up_val, -clamp_limit, clamp_limit)
    activated = ((up_val + 1.0) * gate_val * jax.nn.sigmoid(glu_alpha * gate_val)).astype(
        jnp.bfloat16
    )
    activated = lax.optimization_barrier(activated)
    partials = jnp.einsum(
        "rh,hjf->jrf",
        activated,
        expert_down[0].reshape(expert_down.shape[1], mp_devs, -1),
        preferred_element_type=jnp.float32,
    )
    expert_out = lax.psum_scatter(
        partials.astype(jnp.bfloat16), "mp", scatter_dimension=0, tiled=True
    ).reshape(expert_count, capacity, -1)
    local_width = expert_out.shape[2]
    returned = lax.all_to_all(expert_out, "expert", split_axis=0, concat_axis=0, tiled=True)
    slot_pick = (
        target[:, None] == jnp.arange(expert_count * capacity, dtype=jnp.int32)[None, :]
    ).astype(jnp.bfloat16)
    picked = jnp.dot(
        slot_pick,
        returned.reshape(expert_count * capacity, local_width),
        preferred_element_type=jnp.float32,
    ).reshape(tok_count, top_count, local_width)
    moe_sum = jnp.sum(picked.astype(jnp.float32) * route_weights[0][..., None], axis=1)
    hidden = (first_out.astype(jnp.float32) + moe_sum).astype(jnp.bfloat16)
    return (hidden[None], key_rotary[None], value_fresh[None])


def solution(mesh):
    placed = (
        P("batch", "expert", "mp"),
        P("batch", None),
        P(),
        P("expert", "mp"),
        P("expert", "mp"),
        P("expert", "mp"),
        P("mp", "expert"),
        P("mp"),
        P(),
        P("expert", None, None, "mp"),
        P("expert", "mp", None),
        P("batch", "expert", None),
        P("batch", "expert", None),
    )
    return jax.shard_map(
        shards,
        mesh=mesh,
        in_specs=placed,
        out_specs=(
            P("batch", "expert", "mp"),
            P("batch", "expert", "mp"),
            P("batch", "expert", "mp"),
        ),
        check_vma=False,
    )
```

profile of v0, /device:TPU:1, one launch (start us, length us, event | category | flops | bytes accessed | tf_op | source)
XLA Modules:
  0.0 365.3 jit_solution(1830637323441085088)
XLA Ops:
  10.9 5.9 %all-to-all-start = ((bf16[8,360,128]{2,1,0:T(8,128)(2,1)}), bf16[8,360,128]{2,1,0:T(8,128)(2,1)S(1)}, u32[]{:S(2)}, u32[]{:S(2)}) async-start(bf16[8,360,128]{2,1,0:T(8,128)(2,1)} %broadcast_in_dim.29), calls=%async_computation | async-start | bytes 1474560 | tf_op jit(solution)/shard_map/all_to_all | solution.py:42
  20.5 8.8 %all-to-all-done = bf16[8,360,128]{2,1,0:T(8,128)(2,1)S(1)} async-done(((bf16[8,360,128]{2,1,0:T(8,128)(2,1)}), bf16[8,360,128]{2,1,0:T(8,128)(2,1)S(1)}, u32[]{:S(2)}, u32[]{:S(2)}) %all-to-all-start) | async-done | bytes 737312 | tf_op jit(solution)/shard_map/all_to_all | solution.py:42
  30.2 10.6 %all-to-all-start.1 = ((bf16[16,180,128]{2,1,0:T(8,128)(2,1)}), bf16[16,180,128]{2,1,0:T(8,128)(2,1)S(1)}, u32[]{:S(2)}, u32[]{:S(2)}) async-start(bf16[16,180,128]{2,1,0:T(8,128)(2,1)} %broadcast_in_dim.30), calls=%async_computation.1 | async-start | bytes 1507328 | tf_op jit(solution)/shard_map/all_to_all | solution.py:42
  43.0 26.1 %all-to-all-done.1 = bf16[16,180,128]{2,1,0:T(8,128)(2,1)S(1)} async-done(((bf16[16,180,128]{2,1,0:T(8,128)(2,1)}), bf16[16,180,128]{2,1,0:T(8,128)(2,1)S(1)}, u32[]{:S(2)}, u32[]{:S(2)}) %all-to-all-start.1) | async-done | bytes 737312 | tf_op jit(solution)/shard_map/all_to_all | solution.py:42
  70.9 4.6 %all-to-all-start.2 = ((bf16[16,128,128]{2,1,0:T(8,128)(2,1)}), bf16[16,128,128]{2,1,0:T(8,128)(2,1)S(1)}, u32[]{:S(2)}, u32[]{:S(2)}) async-start(bf16[16,128,128]{2,1,0:T(8,128)(2,1)} %broadcast_in_dim.35), calls=%async_computation.2 | async-start | bytes 1048576 | tf_op jit(solution)/shard_map/all_to_all | solution.py:42
  77.6 66.0 %all-gather.6.cloned.1.call-done = bf16[2944,1024]{1,0:T(8,128)(2,1)} async-done(((bf16[184,1024]{1,0:T(8,128)(2,1)}), bf16[2944,1024]{1,0:T(8,128)(2,1)}) %all-gather.6.cloned.1.call-update) | async-done | bytes 6029328 | tf_op jit(solution)/shard_map/all_gather | solution.py:83
  143.6 3.7 %slice.73 = bf16[16,184,512]{2,1,0:T(8,128)(2,1)} slice(bf16[16,184,1024]{2,1,0:T(8,128)(2,1)} %bitcast.143), slice={[0:16], [0:184], [0:512]} | slice | bytes 6029312 | tf_op jit(solution)/shard_map/slice | solution.py:90
  147.3 3.3 copy.38
  153.7 3.7 %fusion.4 = (f32[1024]{0:T(1024)S(1)}, f32[1024,2048]{1,0:T(8,128)S(1)}) fusion(s32[2048]{0:T(1024)} %bitcast.159, s32[1024]{0:T(1024)} %get-tuple-element.62, s32[1024]{0:T(1024)} %get-tuple-element.61, bf16[2048,128]{1,0:T(8,128)(2,1)S(1)} %bitcast.141, bf16[8,8,8,128]{3,2,1,0:T(8,128)(2,1)S(1)} %bitcast.152), kind=kOutput, calls=%fused_computation.11 | convolution fusion | flops 281017344 | bytes 9064448 | tf_op jit(solution)/shard_map/while/body/eval_jaxpr/hrd,hkd->hrk/dot_general | solution.py:139
  157.5 3.5 convert_reduce_fusion
  164.7 4.0 %all-to-all-start.3 = ((bf16[8,360,128]{2,1,0:T(8,128)(2,1)}), bf16[8,360,128]{2,1,0:T(8,128)(2,1)S(1)}, u32[]{:S(2)}, u32[]{:S(2)}) async-start(bf16[8,360,128]{2,1,0:T(8,128)(2,1)} %reshape.428), calls=%async_computation.3 | async-start | bytes 1474560 | tf_op jit(solution)/shard_map/all_to_all | solution.py:181
  169.0 2.4 scatter_custom_fusion
  171.5 9.7 %all-to-all-done.3 = bf16[8,360,128]{2,1,0:T(8,128)(2,1)S(1)} async-done(((bf16[8,360,128]{2,1,0:T(8,128)(2,1)}), bf16[8,360,128]{2,1,0:T(8,128)(2,1)S(1)}, u32[]{:S(2)}, u32[]{:S(2)}) %all-to-all-start.3) | async-done | bytes 737312 | tf_op jit(solution)/shard_map/all_to_all | solution.py:181
  182.1 22.0 %all_to_all.30 = bf16[16,48,360]{2,1,0:T(8,128)(2,1)S(1)} all-to-all(bf16[16,48,360]{2,1,0:T(8,128)(2,1)S(1)} %bitcast.138), channel_id=1, replica_groups=mesh['expert'=16,'mp'=8,'batch'=2] {'expert'}, dimensions={0} | all-to-all | bytes 1105920 | tf_op jit(solution)/shard_map/all_to_all | solution.py:208
  205.3 3.4 copy.60
  208.6 4.6 %slice_bitcast_fusion.1 = (bf16[2880,360]{0,1:T(8,128)(2,1)}, bf16[2880,360]{0,1:T(8,128)(2,1)}) fusion(bf16[1,2,2880,360]{2,3,1,0:T(8,128)(2,1)} %param.22), kind=kLoop, calls=%fused_computation.20 | loop fusion | bytes 8294400 | tf_op jit(solution)/shard_map/squeeze | solution.py:215
  213.2 44.4 %all-gather.4.cloned.1.call-done = bf16[768,2880]{0,1:T(8,128)(2,1)} async-done(((bf16[768,360]{0,1:T(8,128)(2,1)}), bf16[768,2880]{0,1:T(8,128)(2,1)}) %all-gather.4.cloned.1.call-update) | async-done | bytes 4423696 | tf_op jit(solution)/shard_map/all_gather | solution.py:210
  257.6 3.3 fusion
  263.5 3.6 fusion.5
  267.5 4.5 %convert_bitcast_fusion = bf16[8,768,360]{1,2,0:T(8,128)(2,1)} fusion(bf16[360,8,360]{0,2,1:T(8,128)(2,1)S(1)} %bitcast.140, bf16[768,360]{0,1:T(8,128)(2,1)S(1)} %fusion.28), kind=kOutput, calls=%fused_computation.12 | convolution fusion | flops 1594736640 | bytes 7050240 | tf_op jit(solution)/shard_map/rh,hjf->jrf/dot_general | solution.py:225
  272.0 57.1 %reduce-scatter.2.cloned.1.call-done = bf16[1,768,360]{1,2,0:T(8,128)(2,1)} async-done(((bf16[8,768,360]{1,2,0:T(8,128)(2,1)}), bf16[1,768,360]{1,2,0:T(8,128)(2,1)}) %reduce-scatter.2.cloned.1.call-update) | async-done | bytes 552976 | tf_op jit(solution)/shard_map/reduce_scatter | solution.py:231
  329.0 2.1 copy.53
  331.1 9.0 %all-to-all-start.5 = ((bf16[16,48,360]{2,1,0:T(8,128)(2,1)}), bf16[16,48,360]{2,1,0:T(8,128)(2,1)S(1)}, u32[]{:S(2)}, u32[]{:S(2)}) async-start(bf16[16,48,360]{2,1,0:T(8,128)(2,1)} %bitcast.40), calls=%async_computation.6 | async-start | bytes 1179648 | tf_op jit(solution)/shard_map/all_to_all | solution.py:235
  342.3 15.2 %all-to-all-done.5 = bf16[16,48,360]{2,1,0:T(8,128)(2,1)S(1)} async-done(((bf16[16,48,360]{2,1,0:T(8,128)(2,1)}), bf16[16,48,360]{2,1,0:T(8,128)(2,1)S(1)}, u32[]{:S(2)}, u32[]{:S(2)}) %all-to-all-start.5) | async-done | bytes 552992 | tf_op jit(solution)/shard_map/all_to_all | solution.py:235
  (112 shorter events, 29.6 us)
Async XLA Ops:
  7.2 35.4 %copy-start.11 = (f32[2880]{0:T(1024)S(1)}, f32[2880]{0:T(1024)}, u32[]{:S(2)}) copy-start(f32[2880]{0:T(1024)} %param.15) | copy-start | bytes 34564
  7.2 136.4 %all-gather.6.cloned.1.call-start = ((), (), s32[]{:S(2)}) async-start(), calls=%async_computation.9 | async-start | bytes 6406144 | tf_op jit(solution)/shard_map/all_gather | solution.py:83
  10.9 18.3 %all-to-all-start = ((bf16[8,360,128]{2,1,0:T(8,128)(2,1)}), bf16[8,360,128]{2,1,0:T(8,128)(2,1)S(1)}, u32[]{:S(2)}, u32[]{:S(2)}) async-start(bf16[8,360,128]{2,1,0:T(8,128)(2,1)} %broadcast_in_dim.29), calls=%async_computation | async-start | bytes 1474560 | tf_op jit(solution)/shard_map/all_to_all | solution.py:42
  17.6 25.0 %copy-start.3 = (s32[1,128,4]{2,1,0:T(8,128)}, s32[1,128,4]{2,1,0:T(8,128)S(1)}, u32[]{:S(2)}) copy-start(s32[1,128,4]{2,1,0:T(8,128)S(1)} %copy.45) | copy-start | bytes 6148
  20.4 55.1 %copy-start.6 = (s32[16,4,128]{2,0,1:T(8,128)}, s32[16,4,128]{2,0,1:T(8,128)S(1)}, u32[]{:S(2)}) copy-start(s32[16,4,128]{2,0,1:T(8,128)S(1)} %reduce-window.6) | copy-start | bytes 98308
  30.2 38.9 %all-to-all-start.1 = ((bf16[16,180,128]{2,1,0:T(8,128)(2,1)}), bf16[16,180,128]{2,1,0:T(8,128)(2,1)S(1)}, u32[]{:S(2)}, u32[]{:S(2)}) async-start(bf16[16,180,128]{2,1,0:T(8,128)(2,1)} %broadcast_in_dim.30), calls=%async_computation.1 | async-start | bytes 1507328 | tf_op jit(solution)/shard_map/all_to_all | solution.py:42
  69.7 6.8 %copy-start.8 = (f32[128,128]{0,1:T(8,128)}, f32[128,128]{0,1:T(8,128)S(1)}, u32[]{:S(2)}) copy-start(f32[128,128]{0,1:T(8,128)S(1)} %fusion.68) | copy-start | bytes 196612
  70.9 82.7 %all-to-all-start.2 = ((bf16[16,128,128]{2,1,0:T(8,128)(2,1)}), bf16[16,128,128]{2,1,0:T(8,128)(2,1)S(1)}, u32[]{:S(2)}, u32[]{:S(2)}) async-start(bf16[16,128,128]{2,1,0:T(8,128)(2,1)} %broadcast_in_dim.35), calls=%async_computation.2 | async-start | bytes 1048576 | tf_op jit(solution)/shard_map/all_to_all | solution.py:42
  75.8 71.5 %copy-start.13 = (s32[16,5]{0,1:T(8,128)}, s32[16,5]{0,1:T(8,128)S(1)}, u32[]{:S(2)}) copy-start(s32[16,5]{0,1:T(8,128)S(1)} %reduce-window.9) | copy-start | bytes 964
  153.7 3.8 %copy-start.9 = (s32[1024]{0:T(1024)S(1)}, s32[1024]{0:T(1024)}, u32[]{:S(2)}) copy-start(s32[1024]{0:T(1024)} %get-tuple-element.61) | copy-start | bytes 12292
  153.7 3.8 %copy-start.10 = (s32[1024]{0:T(1024)S(1)}, s32[1024]{0:T(1024)}, u32[]{:S(2)}) copy-start(s32[1024]{0:T(1024)} %get-tuple-element.62) | copy-start | bytes 12292
  157.5 5.2 %slice-start = ((s8[6029312]{0:T(1024)(128)(4,1)}), s8[4194304]{0:T(1024)(128)(4,1)S(1)}, s32[]{:S(2)}) async-start(s8[6029312]{0:T(1024)(128)(4,1)} %bitcast.144), calls=%async_computation.10 | async-start | bytes 8388608
  157.5 5.2 %slice-start.1 = ((s8[6029312]{0:T(1024)(128)(4,1)}), s8[1835008]{0:T(1024)(128)(4,1)S(1)}, s32[]{:S(2)}) async-start(s8[6029312]{0:T(1024)(128)(4,1)} %bitcast.144), calls=%async_computation.11 | async-start | bytes 3670016
  162.6 6.1 %copy-start.4 = (s32[1,128,4]{2,1,0:T(8,128)S(1)}, s32[1,128,4]{2,1,0:T(8,128)}, u32[]{:S(2)}) copy-start(s32[1,128,4]{2,1,0:T(8,128)} %copy-done.3) | copy-start | bytes 6148
  162.6 6.2 %copy-start.7 = (s32[16,4,128]{2,0,1:T(8,128)S(1)}, s32[16,4,128]{2,0,1:T(8,128)}, u32[]{:S(2)}) copy-start(s32[16,4,128]{2,0,1:T(8,128)} %copy-done.6) | copy-start | bytes 98308
  162.7 6.2 %slice-start.2 = ((s32[16,5]{0,1:T(8,128)}), s32[16,4]{0,1:T(4,128)S(1)}, s32[]{:S(2)}) async-start(s32[16,5]{0,1:T(8,128)} %copy-done.13), calls=%async_computation.12 | async-start | bytes 4096 | tf_op jit(solution)/shard_map/slice.1
  162.7 6.2 %copy-start.14 = (s32[512]{0:T(512)S(1)}, s32[512]{0:T(512)}, u32[]{:S(2)}) copy-start(s32[512]{0:T(512)} %eq.110) | copy-start | bytes 6148
  162.7 18.5 %copy-start.5 = (bf16[1,128,360]{1,2,0:T(8,128)(2,1)S(1)}, bf16[1,128,360]{1,2,0:T(8,128)(2,1)}, u32[]{:S(2)}) copy-start(bf16[1,128,360]{1,2,0:T(8,128)(2,1)} %param.13) | copy-start | bytes 276484
  164.7 16.4 %all-to-all-start.3 = ((bf16[8,360,128]{2,1,0:T(8,128)(2,1)}), bf16[8,360,128]{2,1,0:T(8,128)(2,1)S(1)}, u32[]{:S(2)}, u32[]{:S(2)}) async-start(bf16[8,360,128]{2,1,0:T(8,128)(2,1)} %reshape.428), calls=%async_computation.3 | async-start | bytes 1474560 | tf_op jit(solution)/shard_map/all_to_all | solution.py:181
  168.7 88.9 %all-gather.4.cloned.1.call-start = ((), (), s32[]{:S(2)}) async-start(), calls=%async_computation.7 | async-start | bytes 4976640 | tf_op jit(solution)/shard_map/all_gather | solution.py:210
  205.2 123.8 %reduce-scatter.2.cloned.1.call-start = ((), (), s32[]{:S(2)}) async-start(), calls=%async_computation.8 | async-start | bytes 4976640 | tf_op jit(solution)/shard_map/reduce_scatter | solution.py:231
  213.2 47.8 %copy-start.12 = (f32[2880]{0:T(1024)S(1)}, f32[2880]{0:T(1024)}, u32[]{:S(2)}) copy-start(f32[2880]{0:T(1024)} %param.21) | copy-start | bytes 34564
  271.9 85.5 %copy-start.17 = (f32[1,128,4]{1,2,0:T(4,128)S(1)}, f32[1,128,4]{1,2,0:T(4,128)}, u32[]{:S(2)}) copy-start(f32[1,128,4]{1,2,0:T(4,128)} %param.25) | copy-start | bytes 6148
  331.1 26.4 %all-to-all-start.5 = ((bf16[16,48,360]{2,1,0:T(8,128)(2,1)}), bf16[16,48,360]{2,1,0:T(8,128)(2,1)S(1)}, u32[]{:S(2)}, u32[]{:S(2)}) async-start(bf16[16,48,360]{2,1,0:T(8,128)(2,1)} %bitcast.40), calls=%async_computation.6 | async-start | bytes 1179648 | tf_op jit(solution)/shard_map/all_to_all | solution.py:235
  (5 other events, 14.9 us)
Sparse Core Ops, SparseCore 0:
  10.6 132.9 all-gather.5
  205.3 52.2 all-gather.3
  272.1 56.8 reduce-scatter.1
where the time goes:
time: 366 us; the launch traced here: 365 us
  waiting for transfers between devices  227 us (62%)
  starting transfers between devices  34.2 us (9%)
  local copies, waits for them, and re-layouts  33.1 us (9%)
  blocking collectives  22 us (6%)
  matrix products  17.8 us (5%)
  other arithmetic  16.8 us (5%)
  between operations  14.2 us (4%)
    all_gather x1, waiting for transfers between devices, shards(): lax.all_gather(jnp.pad(jnp.concatenate([w_query, w_out.T], axis=1), ((0,...  66 us
    reduce_scatter x1, waiting for transfers between devices, shards(): lax.psum_scatter(partials.astype(jnp.bfloat16), 'mp', scatter_dimension=0...  57.1 us
    all_gather x1, waiting for transfers between devices, shards(): lax.all_gather(arrived_rows, 'mp', axis=1, tiled=True)  44.4 us
    all_to_all x3, waiting for transfers between devices, gather_by_exchange(): lax.all_to_all(spread, axis_name, split_axis=0, concat_axis=0, tiled=True)  34.9 us
    all_to_all x1, blocking collectives, shards(): lax.all_to_all(outgoing, 'expert', split_axis=0, concat_axis=0, tiled=True)  22 us
    all_to_all x3, starting transfers between devices, gather_by_exchange(): lax.all_to_all(spread, axis_name, split_axis=0, concat_axis=0, tiled=True)  21.1 us
    all_to_all x1, waiting for transfers between devices, shards(): lax.all_to_all(expert_out, 'expert', split_axis=0, concat_axis=0, tiled=T...  15.2 us
    all_to_all x1, waiting for transfers between devices, shards(): lax.all_to_all(out_pieces, 'mp', split_axis=0, concat_axis=0, tiled=True)  9.69 us
  transfers between devices with their start and end apart: 8, of which 7 were waited for; matrix products, arithmetic and copies ran while one was open for 10% of the time, Pallas kernels for 0%

commit v1 on v0

--- a/solution.py
+++ b/solution.py
@@ -207,7 +207,12 @@
     )
     arrived = lax.all_to_all(outgoing, "expert", split_axis=0, concat_axis=0, tiled=True)
     arrived_rows = arrived.reshape(expert_count * capacity, arrived.shape[2])
-    inputs = rms_norm(lax.all_gather(arrived_rows, "mp", axis=1, tiled=True), moe_gain)
+    inputs = rms_norm(
+        jnp.concatenate(
+            lax.all_to_all(jnp.stack([arrived_rows] * lax.axis_size("mp")), "mp", 0, 0), axis=1
+        ),
+        moe_gain,
+    )
     w_in = expert_in[0]
     hidden_cols = w_in.shape[2]
     inputs = lax.optimization_barrier(inputs)

time: 366 us -> 385 us (1.052)
  waiting for transfers between devices: 227 us -> 239 us
  starting transfers between devices: 34.2 us -> 38.4 us
    all_gather x1 -> x0, waiting for transfers between devices: 44.4 us -> none  [shards(): lax.all_gather(arrived_rows, 'mp', axis=1, tiled=True)]
    all_to_all x0 -> x1, waiting for transfers between devices: none -> 44 us  [shards(): lax.all_to_all(jnp.stack([arrived_rows] * lax.axis_size('mp')), 'mp', 0, 0)]
    reduce_scatter x1, waiting for transfers between devices: 57.1 us -> 68.9 us  [shards(): lax.psum_scatter(partials.astype(jnp.bfloat16), 'mp', scatter_dimension=0...]
    all_to_all x0 -> x1, starting transfers between devices: none -> 4.57 us  [shards(): lax.all_to_all(jnp.stack([arrived_rows] * lax.axis_size('mp')), 'mp', 0, 0)]
  transfers between devices with their start and end apart: 8 -> 8, of which waited for: 7 -> 7; matrix products, arithmetic and copies ran while one was open for 10% -> 9% of each run, Pallas kernels for 0% -> 0%
where the time goes in v1:
time: 385 us; the launch traced here: 384 us
  waiting for transfers between devices  239 us (62%)
  starting transfers between devices  38.4 us (10%)
  local copies, waits for them, and re-layouts  34.1 us (9%)
  blocking collectives  21.8 us (6%)
  other arithmetic  18.4 us (5%)
  matrix products  17.8 us (5%)
  between operations  14.6 us (4%)
    reduce_scatter x1, waiting for transfers between devices, shards(): lax.psum_scatter(partials.astype(jnp.bfloat16), 'mp', scatter_dimension=0...  68.9 us
    all_gather x1, waiting for transfers between devices, shards(): lax.all_gather(jnp.pad(jnp.concatenate([w_query, w_out.T], axis=1), ((0,...  65.9 us
    all_to_all x1, waiting for transfers between devices, shards(): lax.all_to_all(jnp.stack([arrived_rows] * lax.axis_size('mp')), 'mp', 0, 0)  44 us
    all_to_all x3, waiting for transfers between devices, gather_by_exchange(): lax.all_to_all(spread, axis_name, split_axis=0, concat_axis=0, tiled=True)  35.3 us
    all_to_all x1, blocking collectives, shards(): lax.all_to_all(outgoing, 'expert', split_axis=0, concat_axis=0, tiled=True)  21.8 us
    all_to_all x3, starting transfers between devices, gather_by_exchange(): lax.all_to_all(spread, axis_name, split_axis=0, concat_axis=0, tiled=True)  20.6 us
    all_to_all x1, waiting for transfers between devices, shards(): lax.all_to_all(expert_out, 'expert', split_axis=0, concat_axis=0, tiled=T...  15.2 us
    all_to_all x1, waiting for transfers between devices, shards(): lax.all_to_all(out_pieces, 'mp', split_axis=0, concat_axis=0, tiled=True)  9.74 us
  transfers between devices with their start and end apart: 8, of which 7 were waited for; matrix products, arithmetic and copies ran while one was open for 9% of the time, Pallas kernels for 0%

profile of v1, /device:TPU:1, one launch (start us, length us, event | category | flops | bytes accessed | tf_op | source)
XLA Modules:
  0.0 384.2 jit_solution(4132506987101161328)
XLA Ops:
  10.9 5.9 %all-to-all-start = ((bf16[8,360,128]{2,1,0:T(8,128)(2,1)}), bf16[8,360,128]{2,1,0:T(8,128)(2,1)S(1)}, u32[]{:S(2)}, u32[]{:S(2)}) async-start(bf16[8,360,128]{2,1,0:T(8,128)(2,1)} %broadcast_in_dim.29), calls=%async_computation | async-start | bytes 1474560 | tf_op jit(solution)/shard_map/all_to_all | solution.py:42
  20.5 8.8 %all-to-all-done = bf16[8,360,128]{2,1,0:T(8,128)(2,1)S(1)} async-done(((bf16[8,360,128]{2,1,0:T(8,128)(2,1)}), bf16[8,360,128]{2,1,0:T(8,128)(2,1)S(1)}, u32[]{:S(2)}, u32[]{:S(2)}) %all-to-all-start) | async-done | bytes 737312 | tf_op jit(solution)/shard_map/all_to_all | solution.py:42
  30.2 10.6 %all-to-all-start.1 = ((bf16[16,180,128]{2,1,0:T(8,128)(2,1)}), bf16[16,180,128]{2,1,0:T(8,128)(2,1)S(1)}, u32[]{:S(2)}, u32[]{:S(2)}) async-start(bf16[16,180,128]{2,1,0:T(8,128)(2,1)} %broadcast_in_dim.30), calls=%async_computation.1 | async-start | bytes 1507328 | tf_op jit(solution)/shard_map/all_to_all | solution.py:42
  43.0 26.5 %all-to-all-done.1 = bf16[16,180,128]{2,1,0:T(8,128)(2,1)S(1)} async-done(((bf16[16,180,128]{2,1,0:T(8,128)(2,1)}), bf16[16,180,128]{2,1,0:T(8,128)(2,1)S(1)}, u32[]{:S(2)}, u32[]{:S(2)}) %all-to-all-start.1) | async-done | bytes 737312 | tf_op jit(solution)/shard_map/all_to_all | solution.py:42
  71.4 4.1 %all-to-all-start.2 = ((bf16[16,128,128]{2,1,0:T(8,128)(2,1)}), bf16[16,128,128]{2,1,0:T(8,128)(2,1)S(1)}, u32[]{:S(2)}, u32[]{:S(2)}) async-start(bf16[16,128,128]{2,1,0:T(8,128)(2,1)} %broadcast_in_dim.35), calls=%async_computation.2 | async-start | bytes 1048576 | tf_op jit(solution)/shard_map/all_to_all | solution.py:42
  77.6 65.9 %all-gather.3.cloned.1.call-done = bf16[2944,1024]{1,0:T(8,128)(2,1)} async-done(((bf16[184,1024]{1,0:T(8,128)(2,1)}), bf16[2944,1024]{1,0:T(8,128)(2,1)}) %all-gather.3.cloned.1.call-update) | async-done | bytes 6029328 | tf_op jit(solution)/shard_map/all_gather | solution.py:83
  143.5 3.8 slice.73
  147.3 3.3 copy.23
  153.7 3.7 fusion.3
  157.5 3.5 convert_reduce_fusion
  164.7 4.1 %all-to-all-start.3 = ((bf16[8,360,128]{2,1,0:T(8,128)(2,1)}), bf16[8,360,128]{2,1,0:T(8,128)(2,1)S(1)}, u32[]{:S(2)}, u32[]{:S(2)}) async-start(bf16[8,360,128]{2,1,0:T(8,128)(2,1)} %reshape.431), calls=%async_computation.3 | async-start | bytes 1474560 | tf_op jit(solution)/shard_map/all_to_all | solution.py:181
  171.6 9.7 %all-to-all-done.3 = bf16[8,360,128]{2,1,0:T(8,128)(2,1)S(1)} async-done(((bf16[8,360,128]{2,1,0:T(8,128)(2,1)}), bf16[8,360,128]{2,1,0:T(8,128)(2,1)S(1)}, u32[]{:S(2)}, u32[]{:S(2)}) %all-to-all-start.3) | async-done | bytes 737312 | tf_op jit(solution)/shard_map/all_to_all | solution.py:181
  182.2 21.8 %all_to_all.35 = bf16[16,48,360]{2,1,0:T(8,128)(2,1)S(1)} all-to-all(bf16[16,48,360]{2,1,0:T(8,128)(2,1)S(1)} %bitcast.146), channel_id=1, replica_groups=mesh['expert'=16,'mp'=8,'batch'=2] {'expert'}, dimensions={0} | all-to-all | bytes 1105920 | tf_op jit(solution)/shard_map/all_to_all | solution.py:208
  206.7 4.6 %all-to-all-start.5 = ((bf16[8,768,360]{1,2,0:T(8,128)(2,1)}), bf16[8,768,360]{1,2,0:T(8,128)(2,1)}, u32[]{:S(2)}, u32[]{:S(2)}) async-start(bf16[8,768,360]{1,2,0:T(8,128)(2,1)} %stack.3), calls=%async_computation.5 | async-start | bytes 8847360 | tf_op jit(solution)/shard_map/all_to_all | solution.py:212
  211.3 3.4 copy.45
  214.7 4.6 %slice_bitcast_fusion.1 = (bf16[2880,360]{0,1:T(8,128)(2,1)}, bf16[2880,360]{0,1:T(8,128)(2,1)}) fusion(bf16[1,2,2880,360]{2,3,1,0:T(8,128)(2,1)} %param.22), kind=kLoop, calls=%fused_computation.19 | loop fusion | bytes 8294400 | tf_op jit(solution)/shard_map/squeeze | solution.py:220
  219.3 44.0 %all-to-all-done.5 = bf16[8,768,360]{1,2,0:T(8,128)(2,1)} async-done(((bf16[8,768,360]{1,2,0:T(8,128)(2,1)}), bf16[8,768,360]{1,2,0:T(8,128)(2,1)}, u32[]{:S(2)}, u32[]{:S(2)}) %all-to-all-start.5) | async-done | bytes 4423712 | tf_op jit(solution)/shard_map/all_to_all | solution.py:212
  263.3 3.2 multiply_reduce_fusion
  266.5 3.2 fusion.1
  270.0 3.6 fusion.4
  274.0 4.5 %convert_bitcast_fusion = bf16[8,768,360]{1,2,0:T(8,128)(2,1)} fusion(bf16[360,8,360]{0,2,1:T(8,128)(2,1)S(1)} %bitcast.148, bf16[768,360]{0,1:T(8,128)(2,1)S(1)} %fusion.27), kind=kOutput, calls=%fused_computation.11 | convolution fusion | flops 1594736640 | bytes 7050240 | tf_op jit(solution)/shard_map/rh,hjf->jrf/dot_general | solution.py:230
  278.6 68.9 %reduce-scatter.2.cloned.1.call-done = bf16[1,768,360]{1,2,0:T(8,128)(2,1)} async-done(((bf16[8,768,360]{1,2,0:T(8,128)(2,1)}), bf16[1,768,360]{1,2,0:T(8,128)(2,1)}) %reduce-scatter.2.cloned.1.call-update) | async-done | bytes 552976 | tf_op jit(solution)/shard_map/reduce_scatter | solution.py:236
  349.7 9.0 %all-to-all-start.6 = ((bf16[16,48,360]{2,1,0:T(8,128)(2,1)}), bf16[16,48,360]{2,1,0:T(8,128)(2,1)S(1)}, u32[]{:S(2)}, u32[]{:S(2)}) async-start(bf16[16,48,360]{2,1,0:T(8,128)(2,1)} %bitcast.42), calls=%async_computation.7 | async-start | bytes 1179648 | tf_op jit(solution)/shard_map/all_to_all | solution.py:240
  360.9 15.2 %all-to-all-done.6 = bf16[16,48,360]{2,1,0:T(8,128)(2,1)S(1)} async-done(((bf16[16,48,360]{2,1,0:T(8,128)(2,1)}), bf16[16,48,360]{2,1,0:T(8,128)(2,1)S(1)}, u32[]{:S(2)}, u32[]{:S(2)}) %all-to-all-start.6) | async-done | bytes 552992 | tf_op jit(solution)/shard_map/all_to_all | solution.py:240
  (110 shorter events, 33.6 us)
Async XLA Ops:
  7.2 35.4 %copy-start.10 = (f32[2880]{0:T(1024)S(1)}, f32[2880]{0:T(1024)}, u32[]{:S(2)}) copy-start(f32[2880]{0:T(1024)} %param.15) | copy-start | bytes 34564
  7.2 136.4 %all-gather.3.cloned.1.call-start = ((), (), s32[]{:S(2)}) async-start(), calls=%async_computation.9 | async-start | bytes 6406144 | tf_op jit(solution)/shard_map/all_gather | solution.py:83
  10.9 18.3 %all-to-all-start = ((bf16[8,360,128]{2,1,0:T(8,128)(2,1)}), bf16[8,360,128]{2,1,0:T(8,128)(2,1)S(1)}, u32[]{:S(2)}, u32[]{:S(2)}) async-start(bf16[8,360,128]{2,1,0:T(8,128)(2,1)} %broadcast_in_dim.29), calls=%async_computation | async-start | bytes 1474560 | tf_op jit(solution)/shard_map/all_to_all | solution.py:42
  17.6 25.0 %copy-start.2 = (s32[1,128,4]{2,1,0:T(8,128)}, s32[1,128,4]{2,1,0:T(8,128)S(1)}, u32[]{:S(2)}) copy-start(s32[1,128,4]{2,1,0:T(8,128)S(1)} %copy.30) | copy-start | bytes 6148
  20.4 55.1 %copy-start.5 = (s32[16,4,128]{2,0,1:T(8,128)}, s32[16,4,128]{2,0,1:T(8,128)S(1)}, u32[]{:S(2)}) copy-start(s32[16,4,128]{2,0,1:T(8,128)S(1)} %reduce-window.6) | copy-start | bytes 98308
  30.2 39.3 %all-to-all-start.1 = ((bf16[16,180,128]{2,1,0:T(8,128)(2,1)}), bf16[16,180,128]{2,1,0:T(8,128)(2,1)S(1)}, u32[]{:S(2)}, u32[]{:S(2)}) async-start(bf16[16,180,128]{2,1,0:T(8,128)(2,1)} %broadcast_in_dim.30), calls=%async_computation.1 | async-start | bytes 1507328 | tf_op jit(solution)/shard_map/all_to_all | solution.py:42
  70.1 6.4 %copy-start.7 = (f32[128,128]{0,1:T(8,128)}, f32[128,128]{0,1:T(8,128)S(1)}, u32[]{:S(2)}) copy-start(f32[128,128]{0,1:T(8,128)S(1)} %fusion.67) | copy-start | bytes 196612
  71.4 82.3 %all-to-all-start.2 = ((bf16[16,128,128]{2,1,0:T(8,128)(2,1)}), bf16[16,128,128]{2,1,0:T(8,128)(2,1)S(1)}, u32[]{:S(2)}, u32[]{:S(2)}) async-start(bf16[16,128,128]{2,1,0:T(8,128)(2,1)} %broadcast_in_dim.35), calls=%async_computation.2 | async-start | bytes 1048576 | tf_op jit(solution)/shard_map/all_to_all | solution.py:42
  75.8 71.6 %copy-start.12 = (s32[16,5]{0,1:T(8,128)}, s32[16,5]{0,1:T(8,128)S(1)}, u32[]{:S(2)}) copy-start(s32[16,5]{0,1:T(8,128)S(1)} %reduce-window.9) | copy-start | bytes 964
  153.7 3.8 copy-start.8
  153.7 3.8 copy-start.9
  157.5 5.2 %slice-start = ((s8[6029312]{0:T(1024)(128)(4,1)}), s8[4194304]{0:T(1024)(128)(4,1)S(1)}, s32[]{:S(2)}) async-start(s8[6029312]{0:T(1024)(128)(4,1)} %bitcast.152), calls=%async_computation.10 | async-start | bytes 8388608
  157.5 5.2 %slice-start.1 = ((s8[6029312]{0:T(1024)(128)(4,1)}), s8[1835008]{0:T(1024)(128)(4,1)S(1)}, s32[]{:S(2)}) async-start(s8[6029312]{0:T(1024)(128)(4,1)} %bitcast.152), calls=%async_computation.11 | async-start | bytes 3670016
  162.6 6.3 %copy-start.3 = (s32[1,128,4]{2,1,0:T(8,128)S(1)}, s32[1,128,4]{2,1,0:T(8,128)}, u32[]{:S(2)}) copy-start(s32[1,128,4]{2,1,0:T(8,128)} %copy-done.2) | copy-start | bytes 6148
  162.6 6.4 %copy-start.6 = (s32[16,4,128]{2,0,1:T(8,128)S(1)}, s32[16,4,128]{2,0,1:T(8,128)}, u32[]{:S(2)}) copy-start(s32[16,4,128]{2,0,1:T(8,128)} %copy-done.5) | copy-start | bytes 98308
  162.7 6.4 %slice-start.2 = ((s32[16,5]{0,1:T(8,128)}), s32[16,4]{0,1:T(4,128)S(1)}, s32[]{:S(2)}) async-start(s32[16,5]{0,1:T(8,128)} %copy-done.12), calls=%async_computation.12 | async-start | bytes 4096 | tf_op jit(solution)/shard_map/slice.1
  162.7 6.4 %copy-start.13 = (s32[512]{0:T(512)S(1)}, s32[512]{0:T(512)}, u32[]{:S(2)}) copy-start(s32[512]{0:T(512)} %eq.110) | copy-start | bytes 6148
  162.7 18.7 %copy-start.4 = (bf16[1,128,360]{1,2,0:T(8,128)(2,1)S(1)}, bf16[1,128,360]{1,2,0:T(8,128)(2,1)}, u32[]{:S(2)}) copy-start(bf16[1,128,360]{1,2,0:T(8,128)(2,1)} %param.13) | copy-start | bytes 276484
  164.7 16.6 %all-to-all-start.3 = ((bf16[8,360,128]{2,1,0:T(8,128)(2,1)}), bf16[8,360,128]{2,1,0:T(8,128)(2,1)S(1)}, u32[]{:S(2)}, u32[]{:S(2)}) async-start(bf16[8,360,128]{2,1,0:T(8,128)(2,1)} %reshape.431), calls=%async_computation.3 | async-start | bytes 1474560 | tf_op jit(solution)/shard_map/all_to_all | solution.py:181
  206.7 56.6 %all-to-all-start.5 = ((bf16[8,768,360]{1,2,0:T(8,128)(2,1)}), bf16[8,768,360]{1,2,0:T(8,128)(2,1)}, u32[]{:S(2)}, u32[]{:S(2)}) async-start(bf16[8,768,360]{1,2,0:T(8,128)(2,1)} %stack.3), calls=%async_computation.5 | async-start | bytes 8847360 | tf_op jit(solution)/shard_map/all_to_all | solution.py:212
  211.3 136.3 %reduce-scatter.2.cloned.1.call-start = ((), (), s32[]{:S(2)}) async-start(), calls=%async_computation.8 | async-start | bytes 4976640 | tf_op jit(solution)/shard_map/reduce_scatter | solution.py:236
  219.3 47.2 %copy-start.11 = (f32[2880]{0:T(1024)S(1)}, f32[2880]{0:T(1024)}, u32[]{:S(2)}) copy-start(f32[2880]{0:T(1024)} %param.21) | copy-start | bytes 34564
  278.6 97.5 %copy-start.16 = (f32[1,128,4]{1,2,0:T(4,128)S(1)}, f32[1,128,4]{1,2,0:T(4,128)}, u32[]{:S(2)}) copy-start(f32[1,128,4]{1,2,0:T(4,128)} %param.25) | copy-start | bytes 6148
  349.7 26.4 %all-to-all-start.6 = ((bf16[16,48,360]{2,1,0:T(8,128)(2,1)}), bf16[16,48,360]{2,1,0:T(8,128)(2,1)S(1)}, u32[]{:S(2)}, u32[]{:S(2)}) async-start(bf16[16,48,360]{2,1,0:T(8,128)(2,1)} %bitcast.42), calls=%async_computation.7 | async-start | bytes 1179648 | tf_op jit(solution)/shard_map/all_to_all | solution.py:240
  (4 other events, 14.3 us)
Sparse Core Ops, SparseCore 0:
  10.6 132.8 all-gather.2
  278.7 68.7 reduce-scatter.1
